TPU v7x, 32 devices: a whole 2x2x4 slice. The times are simulated.
32 devices in a mesh: section: 4 (over y, core), site: 8 (over z, x).
Axes of the slice: x: 2, y: 2, z: 4, core: 2. Of those that a mesh axis runs over, the one named last changes fastest.
Arguments:
- acts: bfloat16 [4, 8, 4096], P('section', 'site'), may hold values from -36 to 36
- patches: bfloat16 [4, 2048, 1024], P('section', 'site'), may hold values from -36 to 36
- site_tiles: int32 [8, 256], replicated, may hold values from 0 to 2047, as said below
- site_count: int32 [8], replicated, may hold values from 128 to 256, as said below
- q_weight: bfloat16 [4, 2048, 4096], P('section', 'site'), may hold values from -0.09375 to 0.09375
- q_gain: float32 [4, 128], P('section'), may hold values from 1 to 2.5
- k_gain: float32 [4, 128], P('section'), may hold values from 1 to 2.5
- tile_in: bfloat16 [4, 1024, 512], P('section', 'site'), may hold values from -0.1875 to 0.1875
- tile_out: bfloat16 [4, 512, 4096], P('section', 'site'), may hold values from -0.25 to 0.25
- out_weight: bfloat16 [4, 2048, 4096], P('section', 'site'), may hold values from -0.125 to 0.125
- ffn_gain: float32 [4, 4096], P('section'), may hold values from 0.25 to 1.75
- gate_weight: bfloat16 [4, 7168, 4096], P('section', 'site'), may hold values from -0.09375 to 0.09375
- up_weight: bfloat16 [4, 7168, 4096], P('section', 'site'), may hold values from -0.09375 to 0.09375
- down_weight: bfloat16 [4, 7168, 4096], P('section', 'site'), may hold values from -0.0625 to 0.0625
Outputs:
- passed: bfloat16 [4, 8, 4096], P('section', 'site')
Inputs may be any that keep to these rules, and one draw needn't show every extreme that they name: `site_tiles`: shard k owns tiles k * 256 to (k + 1) * 256 - 1. Of the live entries (l < site_count[n]) of the one site held by a device, at most 40 name tiles of one shard, and in every device exactly 40 name tiles of some shard. All entries of one device's sites are different tiles. `site_count`: sites n with n % 1 == 0, except site 8 - 1, have all 256 entries live; site 8 - 1 has exactly 128.
All inputs are finite; a program needn't handle non-finite values.
Results may differ from a plain program's by a relative error of at most 0.0055.
Values may be sent and summed in bfloat16 or wider, within the bound.
No kernel may reach another device: no remote copies, remote signals or barrier semaphores. Data moves between devices by JAX's collectives and lax.ppermute only.
A program may use at most 128 MiB of HBM per device.

v0:
```python
import math
import jax
import jax.numpy as jnp
from jax import lax
from jax.sharding import PartitionSpec as P

HEADS = 16
epsilon = 1e-05


def shifted(value, axis, steps):
    count = lax.axis_size(axis)
    pairs = [(source, (source + steps) % count) for source in range(count)]
    return lax.ppermute(value, axis, pairs)


def by_rows(left, weight_rows):
    return lax.dot_general(
        left, weight_rows, (((1,), (1,)), ((), ())), preferred_element_type=jnp.float32
    )


def head_norm(values, gain_row):
    shaped = values.astype(jnp.float32).reshape(values.shape[0], -1, gain_row.shape[0])
    scaled = (
        shaped * lax.rsqrt(jnp.mean(shaped * shaped, axis=-1, keepdims=True) + epsilon) * gain_row
    )
    return scaled.reshape(values.shape[0], -1)


def rms_norm(values, gain_row):
    return (
        values * lax.rsqrt(jnp.mean(values * values, axis=-1, keepdims=True) + epsilon) * gain_row
    )


def encode(tile_rows, weight_in, weight_out, key_gain):
    hidden = jax.nn.gelu(
        jnp.dot(tile_rows, weight_in, preferred_element_type=jnp.float32), approximate=True
    ).astype(jnp.bfloat16)
    keyval = jnp.dot(hidden, weight_out, preferred_element_type=jnp.float32)
    half_width = keyval.shape[1] // 2
    normed_keys = head_norm(keyval[:, :half_width], key_gain)
    return jnp.concatenate([normed_keys, keyval[:, half_width:]], axis=1).astype(jnp.bfloat16)


def shards(
    acts,
    patches,
    site_tiles,
    site_count,
    q_weight,
    q_gain,
    k_gain,
    tile_in,
    tile_out,
    out_weight,
    ffn_gain,
    gate_weight,
    up_weight,
    down_weight,
):
    group_size = lax.axis_size("site")
    my_index = lax.axis_index("site")
    sites_here = acts.shape[1]
    list_width = site_tiles.shape[1]
    tiles_here = patches.shape[1]
    head_size = q_gain.shape[1]
    capacity = max(2, 5 * sites_here * list_width // (4 * group_size))
    current = acts[0]
    weight_in, weight_out = (
        lax.all_gather(tile_in[0], "site", axis=0, tiled=True),
        lax.all_gather(tile_out[0], "site", axis=0, tiled=True),
    )
    slot_index = jnp.arange(list_width, dtype=jnp.int32)
    live_all = slot_index[None, :] < site_count[:, None]
    owner_all = site_tiles // tiles_here
    local_all = site_tiles % tiles_here
    mine_mask = jnp.logical_and(live_all, owner_all == my_index).astype(jnp.int32)
    slot_rank = jnp.cumsum(mine_mask, axis=1) - 1
    targets = jnp.where(
        mine_mask == 1,
        jnp.arange(group_size, dtype=jnp.int32)[:, None] * capacity + slot_rank,
        group_size * capacity,
    )
    send_index = (
        jnp.zeros((group_size * capacity + 1,), jnp.int32)
        .at[targets.reshape(-1)]
        .set(local_all.reshape(-1))
    )
    send_index = send_index[:-1].reshape(group_size, capacity)
    my_tiles = lax.dynamic_slice_in_dim(site_tiles, my_index * sites_here, sites_here, 0)
    my_count = lax.dynamic_slice_in_dim(site_count, my_index * sites_here, sites_here, 0)
    my_live = slot_index[None, :] < my_count[:, None]
    my_owner = (my_tiles // tiles_here).reshape(-1)
    one_hot = jnp.logical_and(
        my_owner[:, None] == jnp.arange(group_size, dtype=jnp.int32)[None, :],
        my_live.reshape(-1)[:, None],
    ).astype(jnp.int32)
    my_rank = jnp.sum(jnp.cumsum(one_hot, axis=0) * one_hot, axis=1) - 1
    fetch_index = jnp.where(my_live.reshape(-1), my_owner * capacity + my_rank, 0)
    encoded = encode(patches[0], weight_in, weight_out, k_gain[0])
    arrived = lax.all_to_all(encoded[send_index], "site", split_axis=0, concat_axis=0, tiled=True)
    pair_kv = arrived.reshape(group_size * capacity, -1)[fetch_index]
    pair_kv = pair_kv.reshape(sites_here, list_width, 2, HEADS, head_size)
    everyone = lax.all_gather(current, "site", axis=0, tiled=True)
    q_part = by_rows(everyone, q_weight[0]).astype(jnp.bfloat16)
    my_queries = lax.all_to_all(q_part, "site", split_axis=0, concat_axis=1, tiled=True)
    queries = head_norm(my_queries, q_gain[0]).astype(jnp.bfloat16)
    query_heads = queries.reshape(sites_here, HEADS, head_size)
    scores = jnp.einsum(
        "nhd,nlhd->nhl", query_heads, pair_kv[:, :, 0], preferred_element_type=jnp.float32
    ) / math.sqrt(head_size)
    exponents = jnp.exp(scores) * my_live.astype(jnp.float32)[:, None, :]
    weights = (exponents / jnp.sum(exponents, axis=-1, keepdims=True)).astype(jnp.bfloat16)
    combined = jnp.einsum(
        "nhl,nlhd->nhd", weights, pair_kv[:, :, 1], preferred_element_type=jnp.float32
    )
    combined = combined.reshape(sites_here, -1).astype(jnp.bfloat16)
    columns = lax.all_to_all(combined, "site", split_axis=1, concat_axis=0, tiled=True)
    residual = current.astype(jnp.float32) + lax.psum_scatter(
        jnp.dot(columns, out_weight[0], preferred_element_type=jnp.float32),
        "site",
        scatter_dimension=0,
        tiled=True,
    )
    normed = rms_norm(residual, ffn_gain[0]).astype(jnp.bfloat16)
    normed_rows = lax.all_gather(normed, "site", axis=0, tiled=True)
    gate_sum = by_rows(normed_rows, gate_weight[0])
    up_sum = by_rows(normed_rows, up_weight[0])
    hidden = (jax.nn.silu(gate_sum) * up_sum).astype(jnp.bfloat16)
    output_rows = (
        residual
        + lax.psum_scatter(
            jnp.dot(hidden, down_weight[0], preferred_element_type=jnp.float32),
            "site",
            scatter_dimension=0,
            tiled=True,
        )
    ).astype(jnp.bfloat16)
    return shifted(output_rows[None], "section", 1)


def solution(mesh):
    return jax.shard_map(
        shards,
        mesh=mesh,
        in_specs=(
            P("section", "site", None),
            P("section", "site", None),
            P(),
            P(),
            P("section", "site", None),
            P("section", None),
            P("section", None),
            P("section", "site", None),
            P("section", "site", None),
            P("section", "site", None),
            P("section", None),
            P("section", "site", None),
            P("section", "site", None),
            P("section", "site", None),
        ),
        out_specs=P("section", "site", None),
        check_vma=False,
    )
```

profile of v0, /device:TPU:0, one launch (start us, length us, event | category | flops | bytes accessed | tf_op | source)
XLA Modules:
  0.0 436.5 jit_solution(14200362407360964330)
XLA Ops:
  8.0 32.7 %all-gather = bf16[8,1,4096]{2,1,0:T(2,128)(2,1)S(1)} all-gather(bf16[1,1,4096]{2,1,0:T(2,128)(2,1)} %param.14), channel_id=2, replica_groups=mesh['section'=4,'site'=8] {'site'}, dimensions={0}, use_global_device_ids=true | all-gather | bytes 73728 | tf_op jit(solution)/shard_map/all_gather | solution.py:106
  40.7 2.2 fusion.23
  44.8 5.4 %all-to-all-start = ((bf16[8,2,128]{2,1,0:T(2,128)(2,1)}), bf16[8,2,128]{2,1,0:T(2,128)(2,1)S(1)}, u32[]{:S(2)}, u32[]{:S(2)}) async-start(bf16[8,2,128]{2,1,0:T(2,128)(2,1)} %reshape.383), calls=%async_computation | async-start | bytes 8192 | tf_op jit(solution)/shard_map/all_to_all | solution.py:108
  51.3 8.0 %scatter_custom_fusion = s32[321]{0:T(512)S(1)} fusion(s32[2048]{0:T(1024)S(1)} %bitcast.159, s32[2048]{0:T(1024)S(1)} %bitcast.158, s32[]{:T(128)} %constant.85.clone.1), kind=kCustom, calls=%fused_computation.118 | custom fusion | bytes 1288 | tf_op jit(solution)/shard_map/scatter | solution.py:89
  59.6 67.3 %all-gather.9.cloned.1.call-done = bf16[1,512,4096]{2,1,0:T(8,128)(2,1)} async-done(((bf16[1,64,4096]{2,1,0:T(8,128)(2,1)}), bf16[1,512,4096]{2,1,0:T(8,128)(2,1)}) %all-gather.9.cloned.1.call-update) | async-done | bytes 4194320 | tf_op jit(solution)/shard_map/all_gather | solution.py:73
  126.9 6.1 %fusion.6 = f32[256,4096]{1,0:T(8,128)} fusion(bf16[1,512,4096]{2,1,0:T(8,128)(2,1)} %all-gather.9.cloned.1.call-done, bf16[1,1024,512]{2,1,0:T(8,128)(2,1)} %all-gather.7.cloned.1.call-done, bf16[1,256,1024]{2,1,0:T(8,128)(2,1)S(1)} %copy-done.1), kind=kOutput, calls=%fused_computation.9 | convolution fusion | flops 1343356928 | bytes 9961472 | tf_op jit(solution)/shard_map/dot_general | solution.py:41
  133.0 1.7 slice.54
  134.7 1.7 multiply_bitcast_fusion
  136.5 1.7 copy.37
  138.2 2.2 reduce_sum.46
  141.2 2.4 fusion.9
  145.1 9.9 %gather_fusion = bf16[320,4096]{1,0:T(8,128)(2,1)} fusion(bf16[256,4096]{1,0:T(8,128)(2,1)} %pad_maximum_fusion, s32[1024]{0:T(1024)S(1)} %pad_clamp_fusion.1), kind=kCustom, calls=%fused_computation | custom fusion | bytes 5244160 | tf_op jit(solution)/shard_map/gather | solution.py:103
  155.1 4.5 %all-to-all-start.1 = ((bf16[8,40,4096]{2,1,0:T(8,128)(2,1)}), bf16[8,40,4096]{2,1,0:T(8,128)(2,1)}, u32[]{:S(2)}, u32[]{:S(2)}) async-start(bf16[8,40,4096]{2,1,0:T(8,128)(2,1)} %bitcast.144), calls=%async_computation.1 | async-start | bytes 5242880 | tf_op jit(solution)/shard_map/all_to_all | solution.py:103
  163.7 54.5 %all-to-all-done.1 = bf16[8,40,4096]{2,1,0:T(8,128)(2,1)} async-done(((bf16[8,40,4096]{2,1,0:T(8,128)(2,1)}), bf16[8,40,4096]{2,1,0:T(8,128)(2,1)}, u32[]{:S(2)}, u32[]{:S(2)}) %all-to-all-start.1) | async-done | bytes 2621472 | tf_op jit(solution)/shard_map/all_to_all | solution.py:103
  218.2 7.3 %gather_fusion.1 = bf16[256,4096]{1,0:T(8,128)(2,1)} fusion(bf16[320,4096]{1,0:T(8,128)(2,1)} %bitcast.16, s32[1024]{0:T(1024)S(1)} %pad_clamp_fusion), kind=kCustom, calls=%fused_computation.1 | custom fusion | bytes 4195328 | tf_op jit(solution)/shard_map/gather | solution.py:104
  225.5 2.1 copy.41
  229.6 9.9 %all_to_all.31 = bf16[8,2,128]{2,1,0:T(2,128)(2,1)S(1)} all-to-all(bf16[8,2,128]{2,1,0:T(2,128)(2,1)S(1)} %reshape.385), channel_id=1, replica_groups=mesh['section'=4,'site'=8] {'site'}, dimensions={0} | all-to-all | bytes 8192 | tf_op jit(solution)/shard_map/all_to_all | solution.py:120
  241.2 66.5 %all-reduce.5.cloned.1.call-done = f32[8,4096]{1,0:T(8,128)} async-done(((f32[8,4096]{1,0:T(8,128)}), f32[8,4096]{1,0:T(8,128)}) %all-reduce.5.cloned.1.call-update) | async-done | bytes 131088
  307.6 2.2 multiply_reduce_fusion
  310.4 30.5 %all-gather.3 = bf16[8,1,4096]{2,1,0:T(2,128)(2,1)S(1)} all-gather(bf16[1,1,4096]{2,1,0:T(2,128)(2,1)S(1)} %convert_bitcast_fusion), channel_id=1, replica_groups=mesh['section'=4,'site'=8] {'site'}, dimensions={0}, use_global_device_ids=true | all-gather | bytes 73728 | tf_op jit(solution)/shard_map/all_gather | solution.py:128
  341.0 5.1 %fusion.4 = f32[8,896]{1,0:T(8,128)S(1)} fusion(bf16[1,896,4096]{2,1,0:T(8,128)(2,1)} %param.25, bf16[8,1,4096]{2,1,0:T(2,128)(2,1)S(1)} %all-gather.3), kind=kOutput, calls=%fused_computation.7 | convolution fusion | flops 58720256 | bytes 7434240 | tf_op jit(solution)/shard_map/dot_general | solution.py:18
  346.1 9.3 %fusion = f32[8,4096]{1,0:T(8,128)} fusion(bf16[1,896,4096]{2,1,0:T(8,128)(2,1)} %param.27, bf16[1,896,4096]{2,1,0:T(8,128)(2,1)} %param.26, f32[8,896]{1,0:T(8,128)S(1)} %fusion.4, bf16[8,1,4096]{2,1,0:T(2,128)(2,1)S(1)} %all-gather.3), kind=kOutput, calls=%fused_computation.3 | convolution fusion | flops 117483520 | bytes 14905344 | tf_op jit(solution)/shard_map/dot_general | solution.py:135
  355.4 69.1 %all-reduce.7.cloned.1.call-done = f32[8,4096]{1,0:T(8,128)} async-done(((f32[8,4096]{1,0:T(8,128)}), f32[8,4096]{1,0:T(8,128)}) %all-reduce.7.cloned.1.call-update) | async-done | bytes 131088
  426.2 3.2 collective-permute-done
  (87 shorter events, 16.8 us)
Async XLA Ops:
  6.5 232.9 %copy-start = (bf16[1,256,4096]{2,1,0:T(8,128)(2,1)S(1)}, bf16[1,256,4096]{2,1,0:T(8,128)(2,1)}, u32[]{:S(2)}) copy-start(bf16[1,256,4096]{2,1,0:T(8,128)(2,1)} %param.23) | copy-start | bytes 6291460
  6.5 43.7 %copy-start.3 = (s32[8,256]{1,0:T(8,128)S(1)}, s32[8,256]{1,0:T(8,128)}, u32[]{:S(2)}) copy-start(s32[8,256]{1,0:T(8,128)} %param.16) | copy-start | bytes 24580
  6.5 43.7 %copy-start.6 = (s32[8]{0:T(128)S(1)}, s32[8]{0:T(128)}, u32[]{:S(2)}) copy-start(s32[8]{0:T(128)} %param.17) | copy-start | bytes 100
  6.5 53.0 %copy-start.5 = (f32[1,128]{1,0:T(1,128)S(1)}, f32[1,128]{1,0:T(1,128)}, u32[]{:S(2)}) copy-start(f32[1,128]{1,0:T(1,128)} %param.20) | copy-start | bytes 1540
  6.5 120.3 %copy-start.1 = (bf16[1,256,1024]{2,1,0:T(8,128)(2,1)S(1)}, bf16[1,256,1024]{2,1,0:T(8,128)(2,1)}, u32[]{:S(2)}) copy-start(bf16[1,256,1024]{2,1,0:T(8,128)(2,1)} %param.15) | copy-start | bytes 1572868
  6.5 53.0 %all-gather.7.cloned.1.call-start = ((), (), s32[]{:S(2)}) async-start(), calls=%async_computation.3 | async-start | bytes 1179648 | tf_op jit(solution)/shard_map/all_gather | solution.py:72
  7.3 119.6 %all-gather.9.cloned.1.call-start = ((), (), s32[]{:S(2)}) async-start(), calls=%async_computation.4 | async-start | bytes 4718592 | tf_op jit(solution)/shard_map/all_gather | solution.py:73
  44.8 110.3 %all-to-all-start = ((bf16[8,2,128]{2,1,0:T(2,128)(2,1)}), bf16[8,2,128]{2,1,0:T(2,128)(2,1)S(1)}, u32[]{:S(2)}, u32[]{:S(2)}) async-start(bf16[8,2,128]{2,1,0:T(2,128)(2,1)} %reshape.383), calls=%async_computation | async-start | bytes 8192 | tf_op jit(solution)/shard_map/all_to_all | solution.py:108
  155.1 8.5 %copy-start.7 = (f32[1,128]{1,0:T(1,128)S(1)}, f32[1,128]{1,0:T(1,128)}, u32[]{:S(2)}) copy-start(f32[1,128]{1,0:T(1,128)} %param.19) | copy-start | bytes 1540
  155.1 63.1 %all-to-all-start.1 = ((bf16[8,40,4096]{2,1,0:T(8,128)(2,1)}), bf16[8,40,4096]{2,1,0:T(8,128)(2,1)}, u32[]{:S(2)}, u32[]{:S(2)}) async-start(bf16[8,40,4096]{2,1,0:T(8,128)(2,1)} %bitcast.144), calls=%async_computation.1 | async-start | bytes 5242880 | tf_op jit(solution)/shard_map/all_to_all | solution.py:103
  159.6 148.0 %all-reduce.5.cloned.1.call-start = ((), (), s32[]{:S(2)}) async-start(), calls=%async_computation.5 | async-start | bytes 262144
  227.9 12.7 %copy-start.8 = (u32[32]{0:T(128)S(1)}, u32[32]{0:T(128)}, u32[]{:S(2)}) copy-start(u32[32]{0:T(128)} %constant.112) | copy-start | bytes 388
  227.9 79.7 %copy-start.2 = (bf16[1,1,4096]{2,1,0:T(2,128)(2,1)S(1)}, bf16[1,1,4096]{2,1,0:T(2,128)(2,1)}, u32[]{:S(2)}) copy-start(bf16[1,1,4096]{2,1,0:T(2,128)(2,1)} %param.14) | copy-start | bytes 24580
  227.9 82.5 %copy-start.4 = (f32[1,4096]{1,0:T(1,128)S(1)}, f32[1,4096]{1,0:T(1,128)}, u32[]{:S(2)}) copy-start(f32[1,4096]{1,0:T(1,128)} %param.24) | copy-start | bytes 49156
  240.5 184.1 %all-reduce.7.cloned.1.call-start = ((), (), s32[]{:S(2)}) async-start(), calls=%async_computation.6 | async-start | bytes 262144
  426.1 3.2 collective-permute-start
Sparse Core Ops, SparseCore 0:
  9.5 42.8 all-gather.6
  54.6 72.2 all-gather.8
  240.6 66.9 all-reduce.4
  355.6 68.9 all-reduce.6
where the time goes:
time: 437 us; the launch traced here: 436 us
  waiting for transfers between devices  262 us (60%)
  blocking collectives  73.1 us (17%)
  local copies, waits for them, and re-layouts  35.5 us (8%)
  matrix products  24.6 us (6%)
  other arithmetic  16.9 us (4%)
  between operations  14 us (3%)
  starting transfers between devices  10.4 us (2%)
    unnamed x6, waiting for transfers between devices  137 us
    all_gather x1, waiting for transfers between devices, shards(): lax.all_gather(tile_out[0], 'site', axis=0, tiled=True)  67.3 us
    all_to_all x1, waiting for transfers between devices, shards(): lax.all_to_all(encoded[send_index], 'site', split_axis=0, concat_axis=0,...  54.5 us
    all_gather x1, blocking collectives, shards(): everyone = lax.all_gather(current, 'site', axis=0, tiled=True)  32.7 us
    all_gather x1, blocking collectives, shards(): normed_rows = lax.all_gather(normed, 'site', axis=0, tiled=True)  30.5 us
    gather x1, local copies, waits for them, and re-layouts, shards(): encoded[send_index]  9.94 us
    all_to_all x1, blocking collectives, shards(): lax.all_to_all(combined, 'site', split_axis=1, concat_axis=0, tiled=True)  9.88 us
    dot_general x1, matrix products, shards(): jnp.dot(hidden, down_weight[0], preferred_element_type=jnp.float32)  9.34 us
  transfers between devices with their start and end apart: 7, of which 5 were waited for; matrix products, arithmetic and copies ran while one was open for 10% of the time, Pallas kernels for 0%

commit v1 on v0

--- a/solution.py
+++ b/solution.py
@@ -125,7 +125,16 @@
         tiled=True,
     )
     normed = rms_norm(residual, ffn_gain[0]).astype(jnp.bfloat16)
-    normed_rows = lax.all_gather(normed, "site", axis=0, tiled=True)
+    axis_n = lax.axis_size("site")
+    q_next = normed
+    stack_in = [q_next]
+    val2 = sorted(((i, (i + 1) % axis_n) for i in range(axis_n)))
+    for s in [*range(1, axis_n)]:
+        q_next = lax.ppermute(q_next, "site", val2)
+        stack_in.insert(0, q_next)
+    tmp = jnp.concatenate(stack_in, axis=0)
+    far_arr = lax.axis_index("site") + 1
+    normed_rows = jnp.roll(tmp, shift=far_arr * normed.shape[0], axis=0)
     gate_sum = by_rows(normed_rows, gate_weight[0])
     up_sum = by_rows(normed_rows, up_weight[0])
     hidden = (jax.nn.silu(gate_sum) * up_sum).astype(jnp.bfloat16)

time: 437 us -> 450 us (1.030)
  waiting for transfers between devices: 262 us -> 304 us
  blocking collectives: 73.1 us -> 42.6 us
    ppermute x0 -> x7, waiting for transfers between devices: none -> 44.4 us  [shards(): q_next = lax.ppermute(q_next, 'site', val2)]
    all_gather x1 -> x0, blocking collectives: 30.5 us -> none  [shards(): normed_rows = lax.all_gather(normed, 'site', axis=0, tiled=True)]
  transfers between devices with their start and end apart: 7 -> 14, of which waited for: 5 -> 12; matrix products, arithmetic and copies ran while one was open for 10% -> 10% of each run, Pallas kernels for 0% -> 0%
where the time goes in v1:
time: 450 us
  waiting for transfers between devices  304 us (68%)
  blocking collectives  42.6 us (9%)
  local copies, waits for them, and re-layouts  35.9 us (8%)
  matrix products  24.6 us (5%)
  other arithmetic  16.9 us (4%)
  between operations  14 us (3%)
  starting transfers between devices  11.2 us (2%)
    unnamed x6, waiting for transfers between devices  135 us
    all_gather x1, waiting for transfers between devices, shards(): lax.all_gather(tile_out[0], 'site', axis=0, tiled=True)  67.3 us
    all_to_all x1, waiting for transfers between devices, shards(): lax.all_to_all(encoded[send_index], 'site', split_axis=0, concat_axis=0,...  54.5 us
    ppermute x7, waiting for transfers between devices, shards(): q_next = lax.ppermute(q_next, 'site', val2)  44.4 us
    all_gather x1, blocking collectives, shards(): everyone = lax.all_gather(current, 'site', axis=0, tiled=True)  32.7 us
    gather x1, local copies, waits for them, and re-layouts, shards(): encoded[send_index]  9.94 us
    all_to_all x1, blocking collectives, shards(): lax.all_to_all(combined, 'site', split_axis=1, concat_axis=0, tiled=True)  9.88 us
    dot_general x1, matrix products, shards(): jnp.dot(hidden, down_weight[0], preferred_element_type=jnp.float32)  9.36 us
  transfers between devices with their start and end apart: 14, of which 12 were waited for; matrix products, arithmetic and copies ran while one was open for 10% of the time, Pallas kernels for 0%

profile of v1, /device:TPU:0, one launch (start us, length us, event | category | flops | bytes accessed | tf_op | source)
XLA Modules:
  0.0 449.5 jit_solution(5370801234495914777)
XLA Ops:
  8.0 32.7 %all-gather = bf16[8,1,4096]{2,1,0:T(2,128)(2,1)S(1)} all-gather(bf16[1,1,4096]{2,1,0:T(2,128)(2,1)} %param.14), channel_id=2, replica_groups=mesh['section'=4,'site'=8] {'site'}, dimensions={0}, use_global_device_ids=true | all-gather | bytes 73728 | tf_op jit(solution)/shard_map/all_gather | solution.py:106
  40.7 2.2 fusion.17
  44.8 5.4 %all-to-all-start = ((bf16[8,2,128]{2,1,0:T(2,128)(2,1)}), bf16[8,2,128]{2,1,0:T(2,128)(2,1)S(1)}, u32[]{:S(2)}, u32[]{:S(2)}) async-start(bf16[8,2,128]{2,1,0:T(2,128)(2,1)} %reshape.381), calls=%async_computation | async-start | bytes 8192 | tf_op jit(solution)/shard_map/all_to_all | solution.py:108
  51.3 8.0 %scatter_custom_fusion = s32[321]{0:T(512)S(1)} fusion(s32[2048]{0:T(1024)S(1)} %bitcast.149, s32[2048]{0:T(1024)S(1)} %bitcast.148, s32[]{:T(128)} %constant.104.clone.1), kind=kCustom, calls=%fused_computation.110 | custom fusion | bytes 1288 | tf_op jit(solution)/shard_map/scatter | solution.py:89
  59.6 67.3 %all-gather.8.cloned.1.call-done = bf16[1,512,4096]{2,1,0:T(8,128)(2,1)} async-done(((bf16[1,64,4096]{2,1,0:T(8,128)(2,1)}), bf16[1,512,4096]{2,1,0:T(8,128)(2,1)}) %all-gather.8.cloned.1.call-update) | async-done | bytes 4194320 | tf_op jit(solution)/shard_map/all_gather | solution.py:73
  126.9 6.1 %fusion.6 = f32[256,4096]{1,0:T(8,128)} fusion(bf16[1,512,4096]{2,1,0:T(8,128)(2,1)} %all-gather.8.cloned.1.call-done, bf16[1,1024,512]{2,1,0:T(8,128)(2,1)} %all-gather.6.cloned.1.call-done, bf16[1,256,1024]{2,1,0:T(8,128)(2,1)S(1)} %copy-done.1), kind=kOutput, calls=%fused_computation.9 | convolution fusion | flops 1343356928 | bytes 9961472 | tf_op jit(solution)/shard_map/dot_general | solution.py:41
  141.2 2.4 fusion.9
  145.1 9.9 %gather_fusion = bf16[320,4096]{1,0:T(8,128)(2,1)} fusion(bf16[256,4096]{1,0:T(8,128)(2,1)} %pad_maximum_fusion, s32[1024]{0:T(1024)S(1)} %pad_clamp_fusion.1), kind=kCustom, calls=%fused_computation | custom fusion | bytes 5244160 | tf_op jit(solution)/shard_map/gather | solution.py:103
  155.1 4.5 %all-to-all-start.1 = ((bf16[8,40,4096]{2,1,0:T(8,128)(2,1)}), bf16[8,40,4096]{2,1,0:T(8,128)(2,1)}, u32[]{:S(2)}, u32[]{:S(2)}) async-start(bf16[8,40,4096]{2,1,0:T(8,128)(2,1)} %bitcast.134), calls=%async_computation.1 | async-start | bytes 5242880 | tf_op jit(solution)/shard_map/all_to_all | solution.py:103
  163.7 54.5 %all-to-all-done.1 = bf16[8,40,4096]{2,1,0:T(8,128)(2,1)} async-done(((bf16[8,40,4096]{2,1,0:T(8,128)(2,1)}), bf16[8,40,4096]{2,1,0:T(8,128)(2,1)}, u32[]{:S(2)}, u32[]{:S(2)}) %all-to-all-start.1) | async-done | bytes 2621472 | tf_op jit(solution)/shard_map/all_to_all | solution.py:103
  218.2 7.3 %gather_fusion.1 = bf16[256,4096]{1,0:T(8,128)(2,1)} fusion(bf16[320,4096]{1,0:T(8,128)(2,1)} %bitcast.16, s32[1024]{0:T(1024)S(1)} %pad_clamp_fusion), kind=kCustom, calls=%fused_computation.1 | custom fusion | bytes 4195328 | tf_op jit(solution)/shard_map/gather | solution.py:104
  229.6 9.9 %all_to_all.31 = bf16[8,2,128]{2,1,0:T(2,128)(2,1)S(1)} all-to-all(bf16[8,2,128]{2,1,0:T(2,128)(2,1)S(1)} %reshape.383), channel_id=1, replica_groups=mesh['section'=4,'site'=8] {'site'}, dimensions={0} | all-to-all | bytes 8192 | tf_op jit(solution)/shard_map/all_to_all | solution.py:120
  241.2 66.5 %all-reduce.5.cloned.1.call-done = f32[8,4096]{1,0:T(8,128)} async-done(((f32[8,4096]{1,0:T(8,128)}), f32[8,4096]{1,0:T(8,128)}) %all-reduce.5.cloned.1.call-update) | async-done | bytes 131088
  311.3 5.7 %collective-permute-done = bf16[1,4096]{1,0:T(2,128)(2,1)S(1)} collective-permute-done((bf16[1,4096]{1,0:T(2,128)(2,1)S(1)}, bf16[1,4096]{1,0:T(2,128)(2,1)S(1)}, u32[]{:S(2)}, u32[]{:S(2)}) %collective-permute-start) | collective-permute-done | bytes 8224 | tf_op jit(solution)/shard_map/ppermute | solution.py:133
  316.9 6.4 %collective-permute-done.1 = bf16[1,4096]{1,0:T(2,128)(2,1)S(1)} collective-permute-done((bf16[1,4096]{1,0:T(2,128)(2,1)S(1)}, bf16[1,4096]{1,0:T(2,128)(2,1)S(1)}, u32[]{:S(2)}, u32[]{:S(2)}) %collective-permute-start.1) | collective-permute-done | bytes 8224 | tf_op jit(solution)/shard_map/ppermute | solution.py:133
  323.4 6.5 %collective-permute-done.2 = bf16[1,4096]{1,0:T(2,128)(2,1)S(1)} collective-permute-done((bf16[1,4096]{1,0:T(2,128)(2,1)S(1)}, bf16[1,4096]{1,0:T(2,128)(2,1)S(1)}, u32[]{:S(2)}, u32[]{:S(2)}) %collective-permute-start.2) | collective-permute-done | bytes 8224 | tf_op jit(solution)/shard_map/ppermute | solution.py:133
  329.9 6.4 %collective-permute-done.3 = bf16[1,4096]{1,0:T(2,128)(2,1)S(1)} collective-permute-done((bf16[1,4096]{1,0:T(2,128)(2,1)S(1)}, bf16[1,4096]{1,0:T(2,128)(2,1)S(1)}, u32[]{:S(2)}, u32[]{:S(2)}) %collective-permute-start.3) | collective-permute-done | bytes 8224 | tf_op jit(solution)/shard_map/ppermute | solution.py:133
  336.3 6.4 %collective-permute-done.4 = bf16[1,4096]{1,0:T(2,128)(2,1)S(1)} collective-permute-done((bf16[1,4096]{1,0:T(2,128)(2,1)S(1)}, bf16[1,4096]{1,0:T(2,128)(2,1)S(1)}, u32[]{:S(2)}, u32[]{:S(2)}) %collective-permute-start.4) | collective-permute-done | bytes 8224 | tf_op jit(solution)/shard_map/ppermute | solution.py:133
  342.8 6.4 %collective-permute-done.5 = bf16[1,4096]{1,0:T(2,128)(2,1)S(1)} collective-permute-done((bf16[1,4096]{1,0:T(2,128)(2,1)S(1)}, bf16[1,4096]{1,0:T(2,128)(2,1)S(1)}, u32[]{:S(2)}, u32[]{:S(2)}) %collective-permute-start.5) | collective-permute-done | bytes 8224 | tf_op jit(solution)/shard_map/ppermute | solution.py:133
  349.2 6.4 %collective-permute-done.6 = bf16[1,4096]{1,0:T(2,128)(2,1)S(1)} collective-permute-done((bf16[1,4096]{1,0:T(2,128)(2,1)S(1)}, bf16[1,4096]{1,0:T(2,128)(2,1)S(1)}, u32[]{:S(2)}, u32[]{:S(2)}) %collective-permute-start.6) | collective-permute-done | bytes 8224 | tf_op jit(solution)/shard_map/ppermute | solution.py:133
  356.0 5.1 %fusion.2 = f32[8,896]{1,0:T(8,128)S(1)} fusion(bf16[1,896,4096]{2,1,0:T(8,128)(2,1)} %param.26, bf16[16,4096]{1,0:T(8,128)(2,1)S(1)} %concatenate.11, s32[]{:T(128)S(6)} %select_n.88), kind=kOutput, calls=%fused_computation.5 | convolution fusion | flops 58720256 | bytes 7434244 | tf_op jit(solution)/shard_map/dot_general | solution.py:18
  361.1 9.4 %fusion = f32[8,4096]{1,0:T(8,128)} fusion(bf16[1,896,4096]{2,1,0:T(8,128)(2,1)} %param.27, f32[8,896]{1,0:T(8,128)S(1)} %fusion.2, bf16[1,896,4096]{2,1,0:T(8,128)(2,1)} %param.25, bf16[16,4096]{1,0:T(8,128)(2,1)S(1)} %concatenate.11, s32[]{:T(128)S(6)} %select_n.88), kind=kOutput, calls=%fused_computation.3 | convolution fusion | flops 117483520 | bytes 14905348 | tf_op jit(solution)/shard_map/dot_general | solution.py:144
  370.5 67.1 %all-reduce.7.cloned.1.call-done = f32[8,4096]{1,0:T(8,128)} async-done(((f32[8,4096]{1,0:T(8,128)}), f32[8,4096]{1,0:T(8,128)}) %all-reduce.7.cloned.1.call-update) | async-done | bytes 131088
  439.2 3.2 collective-permute-done.7
  (101 shorter events, 29.6 us)
Async XLA Ops:
  6.5 232.9 %copy-start = (bf16[1,256,4096]{2,1,0:T(8,128)(2,1)S(1)}, bf16[1,256,4096]{2,1,0:T(8,128)(2,1)}, u32[]{:S(2)}) copy-start(bf16[1,256,4096]{2,1,0:T(8,128)(2,1)} %param.23) | copy-start | bytes 6291460
  6.5 43.7 %copy-start.3 = (s32[8,256]{1,0:T(8,128)S(1)}, s32[8,256]{1,0:T(8,128)}, u32[]{:S(2)}) copy-start(s32[8,256]{1,0:T(8,128)} %param.16) | copy-start | bytes 24580
  6.5 43.7 %copy-start.6 = (s32[8]{0:T(128)S(1)}, s32[8]{0:T(128)}, u32[]{:S(2)}) copy-start(s32[8]{0:T(128)} %param.17) | copy-start | bytes 100
  6.5 53.0 %copy-start.5 = (f32[1,128]{1,0:T(1,128)S(1)}, f32[1,128]{1,0:T(1,128)}, u32[]{:S(2)}) copy-start(f32[1,128]{1,0:T(1,128)} %param.20) | copy-start | bytes 1540
  6.5 120.3 %copy-start.1 = (bf16[1,256,1024]{2,1,0:T(8,128)(2,1)S(1)}, bf16[1,256,1024]{2,1,0:T(8,128)(2,1)}, u32[]{:S(2)}) copy-start(bf16[1,256,1024]{2,1,0:T(8,128)(2,1)} %param.15) | copy-start | bytes 1572868
  6.5 53.0 %all-gather.6.cloned.1.call-start = ((), (), s32[]{:S(2)}) async-start(), calls=%async_computation.3 | async-start | bytes 1179648 | tf_op jit(solution)/shard_map/all_gather | solution.py:72
  7.3 119.6 %all-gather.8.cloned.1.call-start = ((), (), s32[]{:S(2)}) async-start(), calls=%async_computation.4 | async-start | bytes 4718592 | tf_op jit(solution)/shard_map/all_gather | solution.py:73
  44.8 110.3 %all-to-all-start = ((bf16[8,2,128]{2,1,0:T(2,128)(2,1)}), bf16[8,2,128]{2,1,0:T(2,128)(2,1)S(1)}, u32[]{:S(2)}, u32[]{:S(2)}) async-start(bf16[8,2,128]{2,1,0:T(2,128)(2,1)} %reshape.381), calls=%async_computation | async-start | bytes 8192 | tf_op jit(solution)/shard_map/all_to_all | solution.py:108
  155.1 8.5 %copy-start.7 = (f32[1,128]{1,0:T(1,128)S(1)}, f32[1,128]{1,0:T(1,128)}, u32[]{:S(2)}) copy-start(f32[1,128]{1,0:T(1,128)} %param.19) | copy-start | bytes 1540
  155.1 63.1 %all-to-all-start.1 = ((bf16[8,40,4096]{2,1,0:T(8,128)(2,1)}), bf16[8,40,4096]{2,1,0:T(8,128)(2,1)}, u32[]{:S(2)}, u32[]{:S(2)}) async-start(bf16[8,40,4096]{2,1,0:T(8,128)(2,1)} %bitcast.134), calls=%async_computation.1 | async-start | bytes 5242880 | tf_op jit(solution)/shard_map/all_to_all | solution.py:103
  159.6 148.0 %all-reduce.5.cloned.1.call-start = ((), (), s32[]{:S(2)}) async-start(), calls=%async_computation.5 | async-start | bytes 262144
  227.9 12.7 %copy-start.8 = (u32[32]{0:T(128)S(1)}, u32[32]{0:T(128)}, u32[]{:S(2)}) copy-start(u32[32]{0:T(128)} %constant.133) | copy-start | bytes 388
  227.9 79.7 %copy-start.2 = (bf16[1,1,4096]{2,1,0:T(2,128)(2,1)S(1)}, bf16[1,1,4096]{2,1,0:T(2,128)(2,1)}, u32[]{:S(2)}) copy-start(bf16[1,1,4096]{2,1,0:T(2,128)(2,1)} %param.14) | copy-start | bytes 24580
  227.9 82.5 %copy-start.4 = (f32[1,4096]{1,0:T(1,128)S(1)}, f32[1,4096]{1,0:T(1,128)}, u32[]{:S(2)}) copy-start(f32[1,4096]{1,0:T(1,128)} %param.24) | copy-start | bytes 49156
  240.5 197.1 %all-reduce.7.cloned.1.call-start = ((), (), s32[]{:S(2)}) async-start(), calls=%async_computation.6 | async-start | bytes 262144
  310.4 6.5 %collective-permute-start = (bf16[1,4096]{1,0:T(2,128)(2,1)S(1)}, bf16[1,4096]{1,0:T(2,128)(2,1)S(1)}, u32[]{:S(2)}, u32[]{:S(2)}) collective-permute-start(bf16[1,4096]{1,0:T(2,128)(2,1)S(1)} %multiply_convert_fusion.1), channel_id=1, source_target_pairs={{0,1},{1,2},{2,3},{3,4},{4,5},{5,6},{6,7},{7,0},{8,9},{9,10},{10,1... | collective-permute-start | bytes 24584 | tf_op jit(solution)/shard_map/ppermute | solution.py:133
  316.9 6.4 %collective-permute-start.1 = (bf16[1,4096]{1,0:T(2,128)(2,1)S(1)}, bf16[1,4096]{1,0:T(2,128)(2,1)S(1)}, u32[]{:S(2)}, u32[]{:S(2)}) collective-permute-start(bf16[1,4096]{1,0:T(2,128)(2,1)S(1)} %collective-permute-done), channel_id=1, source_target_pairs={{0,1},{1,2},{2,3},{3,4},{4,5},{5,6},{6,7},{7,0},{8,9},{9,10},{10,1... | collective-permute-start | bytes 24584 | tf_op jit(solution)/shard_map/ppermute | solution.py:133
  323.4 6.5 %collective-permute-start.2 = (bf16[1,4096]{1,0:T(2,128)(2,1)S(1)}, bf16[1,4096]{1,0:T(2,128)(2,1)S(1)}, u32[]{:S(2)}, u32[]{:S(2)}) collective-permute-start(bf16[1,4096]{1,0:T(2,128)(2,1)S(1)} %collective-permute-done.1), channel_id=1, source_target_pairs={{0,1},{1,2},{2,3},{3,4},{4,5},{5,6},{6,7},{7,0},{8,9},{9,10},{10,1... | collective-permute-start | bytes 24584 | tf_op jit(solution)/shard_map/ppermute | solution.py:133
  329.9 6.4 %collective-permute-start.3 = (bf16[1,4096]{1,0:T(2,128)(2,1)S(1)}, bf16[1,4096]{1,0:T(2,128)(2,1)S(1)}, u32[]{:S(2)}, u32[]{:S(2)}) collective-permute-start(bf16[1,4096]{1,0:T(2,128)(2,1)S(1)} %collective-permute-done.2), channel_id=1, source_target_pairs={{0,1},{1,2},{2,3},{3,4},{4,5},{5,6},{6,7},{7,0},{8,9},{9,10},{10,1... | collective-permute-start | bytes 24584 | tf_op jit(solution)/shard_map/ppermute | solution.py:133
  336.3 6.4 %collective-permute-start.4 = (bf16[1,4096]{1,0:T(2,128)(2,1)S(1)}, bf16[1,4096]{1,0:T(2,128)(2,1)S(1)}, u32[]{:S(2)}, u32[]{:S(2)}) collective-permute-start(bf16[1,4096]{1,0:T(2,128)(2,1)S(1)} %collective-permute-done.3), channel_id=1, source_target_pairs={{0,1},{1,2},{2,3},{3,4},{4,5},{5,6},{6,7},{7,0},{8,9},{9,10},{10,1... | collective-permute-start | bytes 24584 | tf_op jit(solution)/shard_map/ppermute | solution.py:133
  342.8 6.4 %collective-permute-start.5 = (bf16[1,4096]{1,0:T(2,128)(2,1)S(1)}, bf16[1,4096]{1,0:T(2,128)(2,1)S(1)}, u32[]{:S(2)}, u32[]{:S(2)}) collective-permute-start(bf16[1,4096]{1,0:T(2,128)(2,1)S(1)} %collective-permute-done.4), channel_id=1, source_target_pairs={{0,1},{1,2},{2,3},{3,4},{4,5},{5,6},{6,7},{7,0},{8,9},{9,10},{10,1... | collective-permute-start | bytes 24584 | tf_op jit(solution)/shard_map/ppermute | solution.py:133
  349.2 6.4 %collective-permute-start.6 = (bf16[1,4096]{1,0:T(2,128)(2,1)S(1)}, bf16[1,4096]{1,0:T(2,128)(2,1)S(1)}, u32[]{:S(2)}, u32[]{:S(2)}) collective-permute-start(bf16[1,4096]{1,0:T(2,128)(2,1)S(1)} %collective-permute-done.5), channel_id=1, source_target_pairs={{0,1},{1,2},{2,3},{3,4},{4,5},{5,6},{6,7},{7,0},{8,9},{9,10},{10,1... | collective-permute-start | bytes 24584 | tf_op jit(solution)/shard_map/ppermute | solution.py:133
  439.2 3.2 collective-permute-start.7
Sparse Core Ops, SparseCore 0:
  9.5 42.8 all-gather.5
  54.6 72.2 all-gather.7
  240.6 66.9 all-reduce.4
  370.6 66.9 all-reduce.6
